TPU v7x, 32 devices: a whole 2x2x4 slice. The times are simulated.
32 devices in a mesh: region: 4 (over y, x), col: 8 (over z, core).
Axes of the slice: x: 2, y: 2, z: 4, core: 2. Of those that a mesh axis runs over, the one named last changes fastest.
Arguments:
- tiles: float32 [1536, 128, 128], P(('region', 'col')), may hold values from -0.109375 to 0.109375
- tile_rows: int32 [1536], P(('region', 'col')), may hold values from 0 to 1
- tile_cols: int32 [1536], P(('region', 'col')), may hold values from 0 to 15
- tile_count: int32 [32], P(('region', 'col')), may hold values from 12 to 48, as said below
- rhs: float32 [64, 128], P(('region', 'col')), may hold values from -6 to 6
- base_cost: float32 [64, 128], P(('region', 'col')), may hold values from 0.1 to 1
- upper: float32 [64, 128], P(('region', 'col')), may hold values from 0.5 to 4
- primal: float32 [64, 16, 128], P(('region', 'col')), may hold values from 0 to 1
- dual: float32 [64, 16, 128], P(('region', 'col')), may hold values from 0 to 1
- price_levels: float32 [32, 128], replicated, may hold values from 0.5 to 2
- scenario_ids: int32 [16], replicated, may hold values from 0 to 31
Outputs:
- primal_out: float32 [64, 16, 128], P(('region', 'col'))
- dual_out: float32 [64, 16, 128], P(('region', 'col'))
- weight_out: float32 [16], replicated
Inputs may be any that keep to these rules, and one draw needn't show every extreme that they name: `tile_count`: slots at or past a device's count are padding and hold no part of the matrix; in every draw some device has all 48 slots live.
All inputs are finite; a program needn't handle non-finite values.
Results may differ from a plain program's by a relative error of at most 0.0001.
Values sent between devices are 32-bit elements; how exact they have to be, the bound alone decides.
No kernel may reach another device: no remote copies, remote signals or barrier semaphores. Data moves between devices by JAX's collectives and lax.ppermute only.
A program may use at most 64 MiB of HBM per device.

v0:
```python
import jax
import jax.numpy as jnp
from jax import lax
from jax.sharding import PartitionSpec as P

ITERS = 2


def local(
    tiles,
    tile_rows,
    tile_cols,
    tile_count,
    rhs,
    base_cost,
    upper,
    primal,
    dual,
    price_levels,
    scenario_ids,
):
    hp = lax.Precision.HIGHEST
    ntiles = tiles.shape[0]
    row_blocks = rhs.shape[0]
    own_blocks = base_cost.shape[0]
    scenarios = primal.shape[1]
    lanes = primal.shape[2]
    region_blocks = own_blocks * lax.axis_size("col")
    devices = lax.axis_size(("region", "col"))
    live = (jnp.arange(ntiles, dtype=jnp.int32) < tile_count[0]).astype(jnp.float32)
    row_select = (tile_rows[:, None] == jnp.arange(row_blocks, dtype=jnp.int32)[None, :]).astype(
        jnp.float32
    )
    row_live = row_select * live[:, None]
    col_select = (tile_cols[:, None] == jnp.arange(region_blocks, dtype=jnp.int32)[None, :]).astype(
        jnp.float32
    )
    col_live = col_select * live[:, None]
    choose = (
        scenario_ids[:, None] == jnp.arange(price_levels.shape[0], dtype=jnp.int32)[None, :]
    ).astype(jnp.float32)
    factor = jnp.dot(choose, price_levels, precision=hp)
    cost = base_cost[:, None, :] * factor[None, :, :]
    local_a = jnp.sum(jnp.sum(tiles * tiles, axis=(1, 2)) * live)
    local_c = jnp.sum(cost * cost, axis=(0, 2))
    local_b = jnp.sum(rhs * rhs)
    sq_a, sq_c, sq_b = lax.psum((local_a, local_c, local_b), ("region", "col"))
    eta = 0.5 / jnp.sqrt(sq_a / (lanes * row_blocks * devices))
    weight = jnp.sqrt(sq_c) / jnp.sqrt(sq_b)
    width = scenarios * lanes
    for step in range(ITERS):
        tau = (eta / weight)[None, :, None]
        sigma = (eta * weight)[None, :, None]
        dual_rows = jnp.dot(row_select, dual.reshape(row_blocks, width), precision=hp).reshape(
            ntiles, scenarios, lanes
        )
        contrib = jnp.einsum("tij,tsi->tsj", tiles, dual_rows, precision=hp)
        flat_terms = contrib.reshape(ntiles, width)
        partial_value = jnp.dot(col_live.T, flat_terms, precision=hp).reshape(
            region_blocks, scenarios, lanes
        )
        grad = lax.psum_scatter(partial_value, "col", scatter_dimension=0, tiled=True)
        new_primal = jnp.clip(primal - tau * (cost - grad), 0.0, upper[:, None, :])
        point = 2.0 * new_primal - primal
        region_point = lax.all_gather(point, "col", axis=0, tiled=True)
        selected = jnp.dot(
            col_select, region_point.reshape(region_blocks, width), precision=hp
        ).reshape(ntiles, scenarios, lanes)
        image = jnp.einsum("tij,tsj->tsi", tiles, selected, precision=hp)
        product = jnp.dot(row_live.T, image.reshape(ntiles, width), precision=hp).reshape(
            row_blocks, scenarios, lanes
        )
        new_dual = jnp.maximum(dual + sigma * (rhs[:, None, :] - product), 0.0)
        local_x = jnp.sum((new_primal - primal) ** 2, axis=(0, 2))
        local_y = jnp.sum((new_dual - dual) ** 2, axis=(0, 2))
        step_x = lax.psum(local_x, ("region", "col"))
        step_y = lax.psum(local_y, ("region", "col"))
        weight = jnp.sqrt(weight * jnp.sqrt((step_x + 1e-06) / (step_y + 1e-06)))
        primal, dual = (new_primal, new_dual)
    return (primal, dual, weight)


def solution(mesh):
    placed = (
        P(("region", "col"), None, None),
        P(("region", "col")),
        P(("region", "col")),
        P(("region", "col")),
        P(("region", "col"), None),
        P(("region", "col"), None),
        P(("region", "col"), None),
        P(("region", "col"), None, None),
        P(("region", "col"), None, None),
        P(),
        P(),
    )
    return jax.shard_map(
        local,
        mesh=mesh,
        in_specs=placed,
        out_specs=(P(("region", "col"), None, None), P(("region", "col"), None, None), P()),
        check_vma=False,
    )
```

profile of v0, /device:TPU:10, one launch (start us, length us, event | category | flops | bytes accessed | tf_op | source)
XLA Modules:
  0.0 194.1 jit_solution(15329960555821616585)
XLA Ops:
  7.2 0.0 copy-start
  7.2 0.0 copy-start.1
  7.2 0.0 copy-start.7
  7.2 0.0 reduce-scatter.3.cloned.1.call-start
  8.1 1.2 fusion.37
  9.3 0.0 copy-start.10
  9.3 0.0 copy-start.5
  9.3 0.0 copy-start.9
  9.3 0.0 copy-start.3
  9.3 0.0 copy-start.8
  9.3 4.7 %fusion.18 = f32[48,16,128]{2,1,0:T(8,128)S(1)} fusion(f32[48,128,128]{2,1,0:T(8,128)} %param.11, f32[48,16,128]{2,0,1:T(8,128)S(1)} %fusion.37), kind=kOutput, calls=%fused_computation.23 | convolution fusion | flops 150994944 | bytes 3932160 | tf_op jit(solution)/shard_map/tij,tsi->tsj/dot_general | solution.py:57
  14.1 0.0 copy-done.7
  14.1 0.4 fusion.9
  14.5 0.7 copy.80
  15.2 0.0 reduce-scatter.3.cloned.1.call-update
  15.2 0.0 reduce-scatter.5.cloned.1.call-start
  15.2 0.0 copy-done.1
  15.3 0.5 multiply_reduce_fusion
  15.7 0.0 copy-start.6
  15.7 0.0 copy-start.2
  15.7 0.6 fusion.68
  16.3 0.0 copy-done
  16.3 0.0 copy-done.10
  16.3 0.2 fusion.52
  16.5 0.0 copy-done.5
  16.5 0.1 fusion.26
  16.6 0.0 copy-done.9
  16.6 0.6 multiply_reduce_fusion.5
  17.2 41.5 %all-reduce.2 = (f32[16]{0:T(128)S(1)}, f32[]{:T(128)}, f32[]{:T(128)}) all-reduce(f32[16]{0:T(128)S(1)} %fusion.26, f32[]{:T(128)} %fusion.68, f32[]{:T(128)} %multiply_reduce_fusion.5), channel_id=1, replica_groups=mesh['region'=4,'col'=8] {'region','col'}, use_global_device_ids=true, to_apply=%region_6.0 | all-reduce | flops 18 | bytes 144 | tf_op jit(solution)/shard_map/psum | solution.py:47
  60.2 0.0 reduce-scatter.3.cloned.1.call-done
  60.2 0.0 copy-done.3
  60.2 0.0 copy-done.8
  60.2 0.9 multiply_reduce_fusion.4
  61.1 13.1 %all_gather.6 = f32[16,16,128]{2,1,0:T(8,128)S(1)} all-gather(f32[2,16,128]{2,1,0:T(8,128)S(1)} %multiply_subtract_fusion.3), channel_id=1, replica_groups=mesh['region'=4,'col'=8] {'col'}, dimensions={0}, use_global_device_ids=true | all-gather | bytes 147456 | tf_op jit(solution)/shard_map/all_gather | solution.py:65
  74.2 0.4 fusion.23
  74.6 5.0 %fusion.16 = f32[48,16,128]{2,1,0:T(8,128)S(1)} fusion(f32[48,128,128]{2,1,0:T(8,128)S(1)} %copy-done.1, f32[48,16,128]{2,0,1:T(8,128)S(1)} %fusion.23), kind=kOutput, calls=%fused_computation.21 | convolution fusion | flops 150994944 | bytes 3932160 | tf_op jit(solution)/shard_map/tij,tsj->tsi/dot_general | solution.py:69
  79.5 0.0 copy-done.6
  79.5 0.4 fusion.6
  80.0 0.0 copy-done.2
  80.0 0.2 multiply_reduce_fusion.3
  80.2 0.4 fusion.35
  80.6 2.9 %fusion.14 = f32[48,16,128]{2,1,0:T(8,128)S(1)} fusion(f32[48,128,128]{2,1,0:T(8,128)S(1)} %copy-done.1, f32[48,16,128]{2,0,1:T(8,128)S(1)} %fusion.35), kind=kOutput, calls=%fused_computation.19 | convolution fusion | flops 150994944 | bytes 3932160 | tf_op jit(solution)/shard_map/tij,tsi->tsj/dot_general | solution.py:57
  83.4 0.4 fusion.3
  83.9 0.7 copy.87
  84.5 0.0 reduce-scatter.5.cloned.1.call-update
  84.6 40.5 %all-reduce.1 = (f32[16]{0:T(128)S(1)}, f32[16]{0:T(128)S(1)}) all-reduce(f32[16]{0:T(128)S(1)} %get-tuple-element.30, f32[16]{0:T(128)S(1)} %get-tuple-element.28), channel_id=1, replica_groups=mesh['region'=4,'col'=8] {'region','col'}, use_global_device_ids=true, to_apply=%region_11.12 | all-reduce | flops 32 | bytes 256 | tf_op jit(solution)/shard_map/psum | solution.py:77
  125.1 0.0 reduce-scatter.5.cloned.1.call-done
  125.1 0.9 multiply_reduce_fusion.2
  126.0 0.0 copy-start.4
  126.0 12.4 %all_gather.7 = f32[16,16,128]{2,1,0:T(8,128)S(1)} all-gather(f32[2,16,128]{2,1,0:T(8,128)S(1)} %multiply_subtract_fusion.2), channel_id=1, replica_groups=mesh['region'=4,'col'=8] {'col'}, dimensions={0}, use_global_device_ids=true | all-gather | bytes 147456 | tf_op jit(solution)/shard_map/all_gather | solution.py:65
  138.4 0.4 fusion.20
  138.8 5.0 %fusion.12 = f32[48,16,128]{2,1,0:T(8,128)S(1)} fusion(f32[48,128,128]{2,1,0:T(8,128)S(1)} %copy-done.1, f32[48,16,128]{2,0,1:T(8,128)S(1)} %fusion.20), kind=kOutput, calls=%fused_computation.17 | convolution fusion | flops 150994944 | bytes 3932160 | tf_op jit(solution)/shard_map/tij,tsj->tsi/dot_general | solution.py:69
  143.8 0.4 fusion
  144.2 0.8 multiply_reduce_fusion.1
  145.0 41.7 %all-reduce = (f32[16]{0:T(128)S(1)}, f32[16]{0:T(128)S(1)}) all-reduce(f32[16]{0:T(128)S(1)} %get-tuple-element.24, f32[16]{0:T(128)S(1)} %get-tuple-element.22), channel_id=1, replica_groups=mesh['region'=4,'col'=8] {'region','col'}, use_global_device_ids=true, to_apply=%region_16.17 | all-reduce | flops 32 | bytes 256 | tf_op jit(solution)/shard_map/psum | solution.py:77
  186.7 0.5 multiply_sqrt_fusion
  187.2 0.0 copy-done.4
  (6 shorter events, 0.0 us)
Async XLA Ops:
  7.2 9.2 %copy-start = (f32[32,128]{1,0:T(8,128)S(1)}, f32[32,128]{1,0:T(8,128)}, u32[]{:S(2)}) copy-start(f32[32,128]{1,0:T(8,128)} %param.20) | copy-start | bytes 49156
  7.2 8.1 %copy-start.1 = (f32[48,128,128]{2,1,0:T(8,128)S(1)}, f32[48,128,128]{2,1,0:T(8,128)}, u32[]{:S(2)}) copy-start(f32[48,128,128]{2,1,0:T(8,128)} %param.11) | copy-start | bytes 9437188
  7.2 6.9 %copy-start.7 = (s32[48]{0:T(128)S(1)}, s32[48]{0:T(128)}, u32[]{:S(2)}) copy-start(s32[48]{0:T(128)} %param.13) | copy-start | bytes 580
  7.2 53.0 %reduce-scatter.3.cloned.1.call-start = ((), (), s32[]{:S(2)}) async-start(), calls=%async_computation.2 | async-start | bytes 147456 | tf_op jit(solution)/shard_map/reduce_scatter | solution.py:62
  9.3 7.0 %copy-start.10 = (s32[16]{0:T(128)S(1)}, s32[16]{0:T(128)}, u32[]{:S(2)}) copy-start(s32[16]{0:T(128)} %param.21) | copy-start | bytes 196
  9.3 7.2 %copy-start.5 = (f32[2,128]{1,0:T(2,128)S(1)}, f32[2,128]{1,0:T(2,128)}, u32[]{:S(2)}) copy-start(f32[2,128]{1,0:T(2,128)} %param.16) | copy-start | bytes 3076
  9.3 7.3 %copy-start.9 = (f32[2,128]{1,0:T(2,128)S(1)}, f32[2,128]{1,0:T(2,128)}, u32[]{:S(2)}) copy-start(f32[2,128]{1,0:T(2,128)} %param.15) | copy-start | bytes 3076
  9.3 50.9 %copy-start.3 = (f32[2,16,128]{2,1,0:T(8,128)S(1)}, f32[2,16,128]{2,1,0:T(8,128)}, u32[]{:S(2)}) copy-start(f32[2,16,128]{2,1,0:T(8,128)} %param.18) | copy-start | bytes 49156
  9.3 50.9 %copy-start.8 = (f32[2,128]{1,0:T(2,128)S(1)}, f32[2,128]{1,0:T(2,128)}, u32[]{:S(2)}) copy-start(f32[2,128]{1,0:T(2,128)} %param.17) | copy-start | bytes 3076
  15.2 109.9 %reduce-scatter.5.cloned.1.call-start = ((), (), s32[]{:S(2)}) async-start(), calls=%async_computation.3 | async-start | bytes 147456 | tf_op jit(solution)/shard_map/reduce_scatter | solution.py:62
  15.7 63.8 %copy-start.6 = (s32[48]{0:T(128)S(1)}, s32[48]{0:T(128)}, u32[]{:S(2)}) copy-start(s32[48]{0:T(128)} %param.12) | copy-start | bytes 580
  15.7 64.3 %copy-start.2 = (f32[2,16,128]{2,1,0:T(8,128)S(1)}, f32[2,16,128]{2,1,0:T(8,128)}, u32[]{:S(2)}) copy-start(f32[2,16,128]{2,1,0:T(8,128)} %param.19) | copy-start | bytes 49156
  126.0 61.2 %copy-start.4 = (f32[2,16,128]{2,1,0:T(8,128)}, f32[2,16,128]{2,1,0:T(8,128)S(1)}, u32[]{:S(2)}) copy-start(f32[2,16,128]{2,1,0:T(8,128)S(1)} %get-tuple-element.23) | copy-start | bytes 49156
Sparse Core Ops, SparseCore 0:
  15.3 27.7 reduce-scatter.2
  84.7 26.8 reduce-scatter.4
where the time goes:
time: 195 us; the launch traced here: 194 us
  blocking collectives  149 us (76%)
  matrix products  21.7 us (11%)
  between operations  16.4 us (8%)
  other arithmetic  5.15 us (3%)
    psum x2, blocking collectives, local(): step_y = lax.psum(local_y, ('region', 'col'))  82.2 us
    psum x1, blocking collectives, local(): sq_a, sq_c, sq_b = lax.psum((local_a, local_c, local_b), ('region', 'col'))  41.5 us
    all_gather x2, blocking collectives, local(): region_point = lax.all_gather(point, 'col', axis=0, tiled=True)  25.5 us
    dot_general x2, matrix products, local(): image = jnp.einsum('tij,tsj->tsi', tiles, selected, precision=hp)  9.98 us
    dot_general x2, matrix products, local(): contrib = jnp.einsum('tij,tsi->tsj', tiles, dual_rows, precision=hp)  7.59 us
  transfers between devices with their start and end apart: 2, of which 0 were waited for; matrix products, arithmetic and copies ran while one was open for 1% of the time, Pallas kernels for 0%

commit v1 on v0

--- a/solution.py
+++ b/solution.py
@@ -4,6 +4,27 @@
 from jax.sharding import PartitionSpec as P
 
 ITERS = 2
+
+
+def collect(shard, axis, dim):
+    size, index, rows = (lax.axis_size(axis), lax.axis_index(axis), shard.shape[dim])
+    upward = [(i, (i + 1) % size) for i in range(size)]
+    left = [(i, (i - 1) % size) for i in range(size)]
+    out = jnp.zeros((*shard.shape[:dim], size * rows, *shard.shape[dim + 1 :]), shard.dtype)
+    out = lax.dynamic_update_slice_in_dim(out, shard, index * rows, axis=dim)
+    from_left = from_right = shard
+    middle = size // 2
+    for step in range(1, middle + 1):
+        from_left = lax.ppermute(from_left, axis, upward)
+        out = lax.dynamic_update_slice_in_dim(
+            out, from_left, (index - step) % size * rows, axis=dim
+        )
+        if step < size - middle:
+            from_right = lax.ppermute(from_right, axis, left)
+            out = lax.dynamic_update_slice_in_dim(
+                out, from_right, (index + step) % size * rows, axis=dim
+            )
+    return out
 
 
 def local(
@@ -62,7 +83,7 @@
         grad = lax.psum_scatter(partial_value, "col", scatter_dimension=0, tiled=True)
         new_primal = jnp.clip(primal - tau * (cost - grad), 0.0, upper[:, None, :])
         point = 2.0 * new_primal - primal
-        region_point = lax.all_gather(point, "col", axis=0, tiled=True)
+        region_point = collect(point, "col", 0)
         selected = jnp.dot(
             col_select, region_point.reshape(region_blocks, width), precision=hp
         ).reshape(ntiles, scenarios, lanes)

time: 195 us -> 205 us (1.051)
  blocking collectives: 149 us -> 134 us
  waiting for transfers between devices: 0.07 us -> 14.5 us
  starting transfers between devices: 0.08 us -> 11.2 us
    all_gather x2 -> x0, blocking collectives: 25.5 us -> none  [local(): region_point = lax.all_gather(point, 'col', axis=0, tiled=True)]
    ppermute x0 -> x14, waiting for transfers between devices: none -> 14.5 us  [the longest x8 13.6 us: collect(): from_left = lax.ppermute(from_left, axis, upward)]
    ppermute x0 -> x14, starting transfers between devices: none -> 11.1 us  [the longest x6 10.9 us: collect(): from_right = lax.ppermute(from_right, axis, left)]
    psum x2, blocking collectives: 82.2 us -> 92.1 us  [local(): step_y = lax.psum(local_y, ('region', 'col'))]
  transfers between devices with their start and end apart: 2 -> 16, of which waited for: 0 -> 11; matrix products, arithmetic and copies ran while one was open for 1% -> 1% of each run, Pallas kernels for 0% -> 0%
where the time goes in v1:
time: 205 us; the launch traced here: 204 us
  blocking collectives  134 us (65%)
  matrix products  21.7 us (11%)
  between operations  16.5 us (8%)
  waiting for transfers between devices  14.5 us (7%)
  starting transfers between devices  11.2 us (5%)
  other arithmetic  5.17 us (3%)
    psum x2, blocking collectives, local(): step_y = lax.psum(local_y, ('region', 'col'))  92.1 us
    psum x1, blocking collectives, local(): sq_a, sq_c, sq_b = lax.psum((local_a, local_c, local_b), ('region', 'col'))  41.5 us
    ppermute x8, waiting for transfers between devices, collect(): from_left = lax.ppermute(from_left, axis, upward)  13.6 us
    ppermute x6, starting transfers between devices, collect(): from_right = lax.ppermute(from_right, axis, left)  10.9 us
    dot_general x2, matrix products, local(): image = jnp.einsum('tij,tsj->tsi', tiles, selected, precision=hp)  9.98 us
    dot_general x2, matrix products, local(): contrib = jnp.einsum('tij,tsi->tsj', tiles, dual_rows, precision=hp)  7.59 us
  transfers between devices with their start and end apart: 16, of which 11 were waited for; matrix products, arithmetic and copies ran while one was open for 1% of the time, Pallas kernels for 0%

profile of v1, /device:TPU:10, one launch (start us, length us, event | category | flops | bytes accessed | tf_op | source)
XLA Modules:
  0.0 204.2 jit_solution(16433073791537123829)
XLA Ops:
  7.2 0.0 copy-start
  7.2 0.0 copy-start.1
  7.2 0.0 reduce-scatter.3.cloned.1.call-start
  8.1 1.2 fusion.37
  9.3 0.0 copy-start.10
  9.3 0.0 copy-start.5
  9.3 0.0 copy-start.9
  9.3 0.0 copy-start.3
  9.3 0.0 copy-start.8
  9.3 4.7 %fusion.18 = f32[48,16,128]{2,1,0:T(8,128)S(1)} fusion(f32[48,128,128]{2,1,0:T(8,128)} %param.11, f32[48,16,128]{2,0,1:T(8,128)S(1)} %fusion.37), kind=kOutput, calls=%fused_computation.23 | convolution fusion | flops 150994944 | bytes 3932160 | tf_op jit(solution)/shard_map/tij,tsi->tsj/dot_general | solution.py:78
  14.1 0.4 fusion.9
  14.5 0.7 copy.87
  15.2 0.0 reduce-scatter.3.cloned.1.call-update
  15.2 0.0 reduce-scatter.5.cloned.1.call-start
  15.3 0.5 multiply_reduce_fusion
  15.7 0.0 copy-start.2
  15.7 0.2 fusion.52
  15.9 0.1 fusion.26
  16.1 0.6 fusion.68
  16.7 0.6 multiply_reduce_fusion.5
  17.3 41.5 %all-reduce.2 = (f32[16]{0:T(128)S(1)}, f32[]{:T(128)}, f32[]{:T(128)}) all-reduce(f32[16]{0:T(128)S(1)} %fusion.26, f32[]{:T(128)} %fusion.68, f32[]{:T(128)} %multiply_reduce_fusion.5), channel_id=1, replica_groups=mesh['region'=4,'col'=8] {'region','col'}, use_global_device_ids=true, to_apply=%region_6.0 | all-reduce | flops 18 | bytes 144 | tf_op jit(solution)/shard_map/psum | solution.py:68
  60.2 0.0 reduce-scatter.3.cloned.1.call-done
  60.2 0.9 multiply_reduce_fusion.4
  61.2 0.1 collective-permute-start
  61.2 1.7 collective-permute-start.1
  63.0 1.4 collective-permute-done
  64.4 0.0 collective-permute-done.1
  64.4 2.0 collective-permute-start.3
  66.4 1.1 collective-permute-done.2
  67.6 0.3 collective-permute-done.3
  67.9 1.7 collective-permute-start.5
  69.6 1.1 collective-permute-done.4
  70.7 0.0 collective-permute-start.6
  70.7 0.3 collective-permute-done.5
  71.0 2.9 %collective-permute-done.6 = f32[2,16,128]{2,1,0:T(8,128)S(1)} collective-permute-done((f32[2,16,128]{2,1,0:T(8,128)S(1)}, f32[2,16,128]{2,1,0:T(8,128)S(1)}, u32[]{:S(2)}, u32[]{:S(2)}) %collective-permute-start.6) | collective-permute-done | bytes 16416 | tf_op jit(solution)/shard_map/ppermute | solution.py:18
  73.9 0.4 fusion.23
  74.3 5.0 %fusion.16 = f32[48,16,128]{2,1,0:T(8,128)S(1)} fusion(f32[48,128,128]{2,1,0:T(8,128)S(1)} %copy-done.1, f32[48,16,128]{2,0,1:T(8,128)S(1)} %fusion.23), kind=kOutput, calls=%fused_computation.21 | convolution fusion | flops 150994944 | bytes 3932160 | tf_op jit(solution)/shard_map/tij,tsj->tsi/dot_general | solution.py:90
  79.3 0.4 fusion.6
  79.7 0.2 multiply_reduce_fusion.3
  79.9 0.4 fusion.35
  80.3 2.9 %fusion.14 = f32[48,16,128]{2,1,0:T(8,128)S(1)} fusion(f32[48,128,128]{2,1,0:T(8,128)S(1)} %copy-done.1, f32[48,16,128]{2,0,1:T(8,128)S(1)} %fusion.35), kind=kOutput, calls=%fused_computation.19 | convolution fusion | flops 150994944 | bytes 3932160 | tf_op jit(solution)/shard_map/tij,tsi->tsj/dot_general | solution.py:78
  83.1 0.4 fusion.3
  83.6 0.7 copy.94
  84.3 0.0 reduce-scatter.5.cloned.1.call-update
  84.3 46.6 %all-reduce.1 = (f32[16]{0:T(128)S(1)}, f32[16]{0:T(128)S(1)}) all-reduce(f32[16]{0:T(128)S(1)} %get-tuple-element.29, f32[16]{0:T(128)S(1)} %get-tuple-element.27), channel_id=1, replica_groups=mesh['region'=4,'col'=8] {'region','col'}, use_global_device_ids=true, to_apply=%region_11.12 | all-reduce | flops 32 | bytes 256 | tf_op jit(solution)/shard_map/psum | solution.py:98
  130.9 0.0 reduce-scatter.5.cloned.1.call-done
  131.0 0.9 multiply_reduce_fusion.2
  131.9 0.1 collective-permute-start.7
  132.0 1.7 collective-permute-start.8
  133.7 1.4 collective-permute-done.7
  135.1 0.0 collective-permute-done.8
  135.2 1.7 collective-permute-start.10
  136.9 1.4 collective-permute-done.9
  138.3 0.0 collective-permute-done.10
  138.3 2.0 collective-permute-start.12
  140.3 1.3 collective-permute-done.11
  141.6 0.2 collective-permute-done.12
  141.8 3.0 %collective-permute-done.13 = f32[2,16,128]{2,1,0:T(8,128)S(1)} collective-permute-done((f32[2,16,128]{2,1,0:T(8,128)S(1)}, f32[2,16,128]{2,1,0:T(8,128)S(1)}, u32[]{:S(2)}, u32[]{:S(2)}) %collective-permute-start.13) | collective-permute-done | bytes 16416 | tf_op jit(solution)/shard_map/ppermute | solution.py:18
  144.8 0.4 fusion.20
  145.1 5.0 %fusion.12 = f32[48,16,128]{2,1,0:T(8,128)S(1)} fusion(f32[48,128,128]{2,1,0:T(8,128)S(1)} %copy-done.1, f32[48,16,128]{2,0,1:T(8,128)S(1)} %fusion.20), kind=kOutput, calls=%fused_computation.17 | convolution fusion | flops 150994944 | bytes 3932160 | tf_op jit(solution)/shard_map/tij,tsj->tsi/dot_general | solution.py:90
  150.1 0.4 fusion
  150.6 0.8 multiply_reduce_fusion.1
  151.3 45.5 %all-reduce = (f32[16]{0:T(128)S(1)}, f32[16]{0:T(128)S(1)}) all-reduce(f32[16]{0:T(128)S(1)} %get-tuple-element.21, f32[16]{0:T(128)S(1)} %get-tuple-element.19), channel_id=1, replica_groups=mesh['region'=4,'col'=8] {'region','col'}, use_global_device_ids=true, to_apply=%region_16.17 | all-reduce | flops 32 | bytes 256 | tf_op jit(solution)/shard_map/psum | solution.py:98
  196.9 0.5 multiply_sqrt_fusion
  (41 shorter events, 0.2 us)
Async XLA Ops:
  7.2 8.6 %copy-start = (f32[32,128]{1,0:T(8,128)S(1)}, f32[32,128]{1,0:T(8,128)}, u32[]{:S(2)}) copy-start(f32[32,128]{1,0:T(8,128)} %param.20) | copy-start | bytes 49156
  7.2 8.1 %copy-start.1 = (f32[48,128,128]{2,1,0:T(8,128)S(1)}, f32[48,128,128]{2,1,0:T(8,128)}, u32[]{:S(2)}) copy-start(f32[48,128,128]{2,1,0:T(8,128)} %param.11) | copy-start | bytes 9437188
  7.2 6.9 %copy-start.7 = (s32[48]{0:T(128)S(1)}, s32[48]{0:T(128)}, u32[]{:S(2)}) copy-start(s32[48]{0:T(128)} %param.13) | copy-start | bytes 580
  7.2 53.0 %reduce-scatter.3.cloned.1.call-start = ((), (), s32[]{:S(2)}) async-start(), calls=%async_computation.2 | async-start | bytes 147456 | tf_op jit(solution)/shard_map/reduce_scatter | solution.py:83
  9.3 6.5 %copy-start.10 = (s32[16]{0:T(128)S(1)}, s32[16]{0:T(128)}, u32[]{:S(2)}) copy-start(s32[16]{0:T(128)} %param.21) | copy-start | bytes 196
  9.3 6.6 %copy-start.5 = (f32[2,128]{1,0:T(2,128)S(1)}, f32[2,128]{1,0:T(2,128)}, u32[]{:S(2)}) copy-start(f32[2,128]{1,0:T(2,128)} %param.16) | copy-start | bytes 3076
  9.3 7.4 %copy-start.9 = (f32[2,128]{1,0:T(2,128)S(1)}, f32[2,128]{1,0:T(2,128)}, u32[]{:S(2)}) copy-start(f32[2,128]{1,0:T(2,128)} %param.15) | copy-start | bytes 3076
  9.3 50.9 %copy-start.3 = (f32[2,16,128]{2,1,0:T(8,128)S(1)}, f32[2,16,128]{2,1,0:T(8,128)}, u32[]{:S(2)}) copy-start(f32[2,16,128]{2,1,0:T(8,128)} %param.18) | copy-start | bytes 49156
  9.3 50.9 %copy-start.8 = (f32[2,128]{1,0:T(2,128)S(1)}, f32[2,128]{1,0:T(2,128)}, u32[]{:S(2)}) copy-start(f32[2,128]{1,0:T(2,128)} %param.17) | copy-start | bytes 3076
  15.2 115.7 %reduce-scatter.5.cloned.1.call-start = ((), (), s32[]{:S(2)}) async-start(), calls=%async_computation.3 | async-start | bytes 147456 | tf_op jit(solution)/shard_map/reduce_scatter | solution.py:83
  15.7 63.5 %copy-start.6 = (s32[48]{0:T(128)S(1)}, s32[48]{0:T(128)}, u32[]{:S(2)}) copy-start(s32[48]{0:T(128)} %param.12) | copy-start | bytes 580
  15.7 64.0 %copy-start.2 = (f32[2,16,128]{2,1,0:T(8,128)S(1)}, f32[2,16,128]{2,1,0:T(8,128)}, u32[]{:S(2)}) copy-start(f32[2,16,128]{2,1,0:T(8,128)} %param.19) | copy-start | bytes 49156
  61.2 3.2 %collective-permute-start = (f32[2,16,128]{2,1,0:T(8,128)S(1)}, f32[2,16,128]{2,1,0:T(8,128)S(1)}, u32[]{:S(2)}, u32[]{:S(2)}) collective-permute-start(f32[2,16,128]{2,1,0:T(8,128)S(1)} %get-tuple-element.34), channel_id=1, source_target_pairs={{0,1},{1,2},{2,3},{3,4},{4,5},{5,6},{6,7},{7,0},{8,9},{9,10},{10,1... | collective-permute-start | bytes 49160 | tf_op jit(solution)/shard_map/ppermute | solution.py:18
  61.2 3.2 %collective-permute-start.1 = (f32[2,16,128]{2,1,0:T(8,128)S(1)}, f32[2,16,128]{2,1,0:T(8,128)S(1)}, u32[]{:S(2)}, u32[]{:S(2)}) collective-permute-start(f32[2,16,128]{2,1,0:T(8,128)S(1)} %get-tuple-element.34), channel_id=1, source_target_pairs={{0,7},{1,0},{2,1},{3,2},{4,3},{5,4},{6,5},{7,6},{8,15},{9,8},{10,9... | collective-permute-start | bytes 49160 | tf_op jit(solution)/shard_map/ppermute | solution.py:23
  64.4 3.2 %collective-permute-start.2 = (f32[2,16,128]{2,1,0:T(8,128)S(1)}, f32[2,16,128]{2,1,0:T(8,128)S(1)}, u32[]{:S(2)}, u32[]{:S(2)}) collective-permute-start(f32[2,16,128]{2,1,0:T(8,128)S(1)} %collective-permute-done), channel_id=1, source_target_pairs={{0,1},{1,2},{2,3},{3,4},{4,5},{5,6},{6,7},{7,0},{8,9},{9,10},{10,1... | collective-permute-start | bytes 49160 | tf_op jit(solution)/shard_map/ppermute | solution.py:18
  64.4 3.5 %collective-permute-start.3 = (f32[2,16,128]{2,1,0:T(8,128)S(1)}, f32[2,16,128]{2,1,0:T(8,128)S(1)}, u32[]{:S(2)}, u32[]{:S(2)}) collective-permute-start(f32[2,16,128]{2,1,0:T(8,128)S(1)} %collective-permute-done.1), channel_id=1, source_target_pairs={{0,7},{1,0},{2,1},{3,2},{4,3},{5,4},{6,5},{7,6},{8,15},{9,8},{10,9... | collective-permute-start | bytes 49160 | tf_op jit(solution)/shard_map/ppermute | solution.py:23
  67.6 3.2 %collective-permute-start.4 = (f32[2,16,128]{2,1,0:T(8,128)S(1)}, f32[2,16,128]{2,1,0:T(8,128)S(1)}, u32[]{:S(2)}, u32[]{:S(2)}) collective-permute-start(f32[2,16,128]{2,1,0:T(8,128)S(1)} %collective-permute-done.2), channel_id=1, source_target_pairs={{0,1},{1,2},{2,3},{3,4},{4,5},{5,6},{6,7},{7,0},{8,9},{9,10},{10,1... | collective-permute-start | bytes 49160 | tf_op jit(solution)/shard_map/ppermute | solution.py:18
  67.9 3.2 %collective-permute-start.5 = (f32[2,16,128]{2,1,0:T(8,128)S(1)}, f32[2,16,128]{2,1,0:T(8,128)S(1)}, u32[]{:S(2)}, u32[]{:S(2)}) collective-permute-start(f32[2,16,128]{2,1,0:T(8,128)S(1)} %collective-permute-done.3), channel_id=1, source_target_pairs={{0,7},{1,0},{2,1},{3,2},{4,3},{5,4},{6,5},{7,6},{8,15},{9,8},{10,9... | collective-permute-start | bytes 49160 | tf_op jit(solution)/shard_map/ppermute | solution.py:23
  70.7 3.2 %collective-permute-start.6 = (f32[2,16,128]{2,1,0:T(8,128)S(1)}, f32[2,16,128]{2,1,0:T(8,128)S(1)}, u32[]{:S(2)}, u32[]{:S(2)}) collective-permute-start(f32[2,16,128]{2,1,0:T(8,128)S(1)} %collective-permute-done.4), channel_id=1, source_target_pairs={{0,1},{1,2},{2,3},{3,4},{4,5},{5,6},{6,7},{7,0},{8,9},{9,10},{10,1... | collective-permute-start | bytes 49160 | tf_op jit(solution)/shard_map/ppermute | solution.py:18
  131.9 65.5 %copy-start.4 = (f32[2,16,128]{2,1,0:T(8,128)}, f32[2,16,128]{2,1,0:T(8,128)S(1)}, u32[]{:S(2)}) copy-start(f32[2,16,128]{2,1,0:T(8,128)S(1)} %get-tuple-element.20) | copy-start | bytes 49156
  131.9 3.2 %collective-permute-start.7 = (f32[2,16,128]{2,1,0:T(8,128)S(1)}, f32[2,16,128]{2,1,0:T(8,128)S(1)}, u32[]{:S(2)}, u32[]{:S(2)}) collective-permute-start(f32[2,16,128]{2,1,0:T(8,128)S(1)} %get-tuple-element.26), channel_id=1, source_target_pairs={{0,1},{1,2},{2,3},{3,4},{4,5},{5,6},{6,7},{7,0},{8,9},{9,10},{10,1... | collective-permute-start | bytes 49160 | tf_op jit(solution)/shard_map/ppermute | solution.py:18
  132.0 3.2 %collective-permute-start.8 = (f32[2,16,128]{2,1,0:T(8,128)S(1)}, f32[2,16,128]{2,1,0:T(8,128)S(1)}, u32[]{:S(2)}, u32[]{:S(2)}) collective-permute-start(f32[2,16,128]{2,1,0:T(8,128)S(1)} %get-tuple-element.26), channel_id=1, source_target_pairs={{0,7},{1,0},{2,1},{3,2},{4,3},{5,4},{6,5},{7,6},{8,15},{9,8},{10,9... | collective-permute-start | bytes 49160 | tf_op jit(solution)/shard_map/ppermute | solution.py:23
  135.1 3.2 %collective-permute-start.9 = (f32[2,16,128]{2,1,0:T(8,128)S(1)}, f32[2,16,128]{2,1,0:T(8,128)S(1)}, u32[]{:S(2)}, u32[]{:S(2)}) collective-permute-start(f32[2,16,128]{2,1,0:T(8,128)S(1)} %collective-permute-done.7), channel_id=1, source_target_pairs={{0,1},{1,2},{2,3},{3,4},{4,5},{5,6},{6,7},{7,0},{8,9},{9,10},{10,1... | collective-permute-start | bytes 49160 | tf_op jit(solution)/shard_map/ppermute | solution.py:18
  135.2 3.2 %collective-permute-start.10 = (f32[2,16,128]{2,1,0:T(8,128)S(1)}, f32[2,16,128]{2,1,0:T(8,128)S(1)}, u32[]{:S(2)}, u32[]{:S(2)}) collective-permute-start(f32[2,16,128]{2,1,0:T(8,128)S(1)} %collective-permute-done.8), channel_id=1, source_target_pairs={{0,7},{1,0},{2,1},{3,2},{4,3},{5,4},{6,5},{7,6},{8,15},{9,8},{10,9... | collective-permute-start | bytes 49160 | tf_op jit(solution)/shard_map/ppermute | solution.py:23
  138.3 3.3 %collective-permute-start.11 = (f32[2,16,128]{2,1,0:T(8,128)S(1)}, f32[2,16,128]{2,1,0:T(8,128)S(1)}, u32[]{:S(2)}, u32[]{:S(2)}) collective-permute-start(f32[2,16,128]{2,1,0:T(8,128)S(1)} %collective-permute-done.9), channel_id=1, source_target_pairs={{0,1},{1,2},{2,3},{3,4},{4,5},{5,6},{6,7},{7,0},{8,9},{9,10},{10,1... | collective-permute-start | bytes 49160 | tf_op jit(solution)/shard_map/ppermute | solution.py:18
  138.3 3.5 %collective-permute-start.12 = (f32[2,16,128]{2,1,0:T(8,128)S(1)}, f32[2,16,128]{2,1,0:T(8,128)S(1)}, u32[]{:S(2)}, u32[]{:S(2)}) collective-permute-start(f32[2,16,128]{2,1,0:T(8,128)S(1)} %collective-permute-done.10), channel_id=1, source_target_pairs={{0,7},{1,0},{2,1},{3,2},{4,3},{5,4},{6,5},{7,6},{8,15},{9,8},{10,9... | collective-permute-start | bytes 49160 | tf_op jit(solution)/shard_map/ppermute | solution.py:23
  141.6 3.2 %collective-permute-start.13 = (f32[2,16,128]{2,1,0:T(8,128)S(1)}, f32[2,16,128]{2,1,0:T(8,128)S(1)}, u32[]{:S(2)}, u32[]{:S(2)}) collective-permute-start(f32[2,16,128]{2,1,0:T(8,128)S(1)} %collective-permute-done.11), channel_id=1, source_target_pairs={{0,1},{1,2},{2,3},{3,4},{4,5},{5,6},{6,7},{7,0},{8,9},{9,10},{10,1... | collective-permute-start | bytes 49160 | tf_op jit(solution)/shard_map/ppermute | solution.py:18
Sparse Core Ops, SparseCore 0:
  15.3 27.7 reduce-scatter.2
  84.4 31.3 reduce-scatter.4
